TPU v7x, 512 devices: a whole 4x4x16 slice. The times are simulated.
512 devices in a mesh: row: 16 (over z), col: 32 (over y, x, core).
Axes of the slice: x: 4, y: 4, z: 16, core: 2. Of those that a mesh axis runs over, the one named last changes fastest.
Arguments:
- node_feats: bfloat16 [262144, 512], P(('row', 'col')), may hold values from -8 to 8
- source_feats: bfloat16 [4096, 512], P('col'), may hold values from -6 to 6
- nbr_blocks: int32 [2048, 8], P(('row', 'col')), may hold values from 0 to 31
- nbr_count: int32 [2048], P(('row', 'col')), may hold values from 1 to 8
- adj_tiles: bfloat16 [2048, 8, 128, 128], P(('row', 'col')), may hold values from -0.1875 to 0.1875
- pos_index: int32 [262144], P(('row', 'col')), may hold values from 0 to 511
- noise_block_rows: int32 [16], replicated, may hold values from 0 to 15
- w_self: bfloat16 [512, 512], replicated, may hold values from -0.25 to 0.25
- w_neigh: bfloat16 [512, 512], replicated, may hold values from -0.25 to 0.25
Outputs:
- grad_self: float32 [512, 512], replicated
- neighbour_weight_gradient: float32 [512, 512], replicated
- loss: float32 [], replicated
All inputs are finite; a program needn't handle non-finite values.
Results may differ from a plain program's by a relative error of at most 0.002.
Values may be sent and summed in bfloat16 or wider, within the bound.
No kernel may reach another device: no remote copies, remote signals or barrier semaphores. Data moves between devices by JAX's collectives and lax.ppermute only.
A program may use at most 64 MiB of HBM per device.

v0:
```python
import jax
import jax.numpy as jnp
from jax import lax
from jax.sharding import PartitionSpec as P

BLOCK = 128
NOISE = 128
softness_divisor = 0.2


def embed(pre):
    return pre * lax.rsqrt(jnp.sum(pre * pre, axis=-1, keepdims=True) + 1e-06)


def body(
    node_feats,
    source_feats,
    nbr_blocks,
    nbr_count,
    adj_tiles,
    pos_index,
    noise_block_rows,
    w_self,
    w_neigh,
):
    rows = node_feats.shape[0]
    width = node_feats.shape[1]
    slots = adj_tiles.shape[1]
    highest = lax.Precision.HIGHEST
    nodes = rows * lax.axis_size("row") * lax.axis_size("col")
    scale_factor = 1.0 / softness_divisor
    valid = jnp.arange(slots, dtype=jnp.int32)[None, :] < nbr_count[:, None]
    tiles = adj_tiles * valid[:, :, None, None].astype(jnp.bfloat16)
    piece = lax.all_gather(source_feats, "col", axis=0, tiled=True)
    count = piece.shape[0] // BLOCK
    blocks = piece.reshape(count, BLOCK, width)
    indicator_matrix = (
        nbr_blocks[:, :, None] == jnp.arange(count, dtype=jnp.int32)[None, None, :]
    ).astype(jnp.bfloat16)
    selected = jnp.einsum(
        "bkc,cjd->bkjd", indicator_matrix, blocks, preferred_element_type=jnp.float32
    ).astype(jnp.bfloat16)
    summed = jnp.einsum("bkij,bkjd->bid", tiles, selected, preferred_element_type=jnp.float32)
    agg = summed.reshape(rows, width).astype(jnp.bfloat16)
    pre = jnp.dot(node_feats, w_self, preferred_element_type=jnp.float32) + jnp.dot(
        agg, w_neigh, preferred_element_type=jnp.float32
    )
    emb32, pull = jax.vjp(embed, pre)
    zeta_bf = emb32.astype(jnp.bfloat16)
    candidates = lax.all_gather(zeta_bf[:NOISE], "row", axis=0, tiled=True)
    my_row = lax.axis_index("row")
    my_noise = noise_block_rows[my_row]
    noise_emb = lax.dynamic_slice_in_dim(candidates, my_noise * NOISE, NOISE, 0).astype(jnp.float32)
    zeta = zeta_bf.astype(jnp.float32)
    pairing = (pos_index[:, None] == jnp.arange(rows, dtype=jnp.int32)[None, :]).astype(jnp.float32)
    partner = jnp.dot(pairing, zeta, precision=highest)
    s_pos = jnp.sum(zeta * partner, axis=-1) * scale_factor
    s_neg = jnp.dot(zeta, noise_emb.T, precision=highest) * scale_factor
    loss_part = (jnp.sum(jax.nn.softplus(-s_pos)) + jnp.sum(jax.nn.softplus(s_neg)) / NOISE) / nodes
    grad_pos = -jax.nn.sigmoid(-s_pos) / nodes
    grad_neg = jax.nn.sigmoid(s_neg) / (NOISE * nodes)
    anchor = scale_factor * (
        grad_pos[:, None] * partner + jnp.dot(grad_neg, noise_emb, precision=highest)
    )
    partner_grad = jnp.dot(pairing.T, scale_factor * grad_pos[:, None] * zeta, precision=highest)
    dnoise = scale_factor * jnp.dot(grad_neg.T, zeta, precision=highest)
    groups = lax.axis_size("row")
    collected = lax.all_gather(dnoise.astype(jnp.bfloat16), "row", axis=0, tiled=True)
    owned = (noise_block_rows == my_row).astype(jnp.float32)
    returned = jnp.dot(
        owned[None, :],
        collected.astype(jnp.float32).reshape(groups, NOISE * width),
        precision=highest,
    )
    returned = returned.reshape(NOISE, width)
    dzeta = anchor + partner_grad
    dzeta = dzeta.at[:NOISE].add(returned)
    gpre = pull(dzeta)[0].astype(jnp.bfloat16)
    part_self = jnp.dot(node_feats.T, gpre, preferred_element_type=jnp.float32)
    neighbour_partial = jnp.dot(agg.T, gpre, preferred_element_type=jnp.float32)
    grad_self, neighbour_weight_gradient, loss = lax.psum(
        (part_self, neighbour_partial, loss_part), ("row", "col")
    )
    return (grad_self, neighbour_weight_gradient, loss)


def solution(mesh):
    in_specs = (
        P(("row", "col"), None),
        P("col", None),
        P(("row", "col"), None),
        P(("row", "col")),
        P(("row", "col"), None, None, None),
        P(("row", "col")),
        P(),
        P(),
        P(),
    )
    out_specs = (P(), P(), P())
    return jax.shard_map(body, mesh=mesh, in_specs=in_specs, out_specs=out_specs, check_vma=False)
```

profile of v0, /device:TPU:1, one launch (start us, length us, event | category | flops | bytes accessed | tf_op | source)
XLA Modules:
  0.0 734.0 jit_solution(15400814606287364603)
XLA Ops:
  7.2 0.7 all-gather.4.cloned.1.call-update
  8.0 0.7 fusion.26
  8.7 1.5 fusion.36
  10.2 68.1 %all-gather.4.cloned.1.call-done = bf16[4096,512]{1,0:T(8,128)(2,1)} async-done(((bf16[128,512]{1,0:T(8,128)(2,1)}), bf16[4096,512]{1,0:T(8,128)(2,1)}) %all-gather.4.cloned.1.call-update) | async-done | bytes 4194320 | tf_op jit(solution)/shard_map/all_gather | solution.py:34
  78.3 5.6 fusion.1
  83.9 2.6 fusion.8
  87.4 0.7 slice.24
  88.2 0.6 dynamic_slice.6
  89.4 66.7 %all-gather.6.cloned.1.call-done = bf16[2048,512]{0,1:T(8,128)(2,1)} async-done(((bf16[128,512]{0,1:T(8,128)(2,1)}), bf16[2048,512]{0,1:T(8,128)(2,1)}) %all-gather.6.cloned.1.call-update) | async-done | bytes 2097168 | tf_op jit(solution)/shard_map/all_gather | solution.py:50
  156.1 1.9 fusion.18
  158.0 1.4 fusion.9
  159.7 0.6 fusion.10
  160.3 0.6 fusion.25
  160.9 1.6 fusion.7
  162.5 1.2 convolution_add_fusion.1
  163.7 66.2 %all-gather.8.cloned.1.call-done = bf16[2048,512]{1,0:T(8,128)(2,1)} async-done(((bf16[128,512]{1,0:T(8,128)(2,1)}), bf16[2048,512]{1,0:T(8,128)(2,1)}) %all-gather.8.cloned.1.call-update) | async-done | bytes 2097168 | tf_op jit(solution)/shard_map/all_gather | solution.py:68
  229.9 3.2 reshape.99
  233.1 2.0 fusion.3
  235.9 2.5 fusion.37
  238.4 1.4 convolution_bitcast_fusion
  241.1 110.9 %psum.23 = f32[]{:T(128)} all-reduce(f32[]{:T(128)S(6)} %div.45), channel_id=1, replica_groups=mesh['row'=16,'col'=32] {'row','col'}, use_global_device_ids=true, to_apply=%region_7.8 | all-reduce | flops 1 | bytes 8 | tf_op jit(solution)/shard_map/psum | solution.py:81
  351.9 370.7 %all-reduce.3.cloned.1.call-done = (f32[512,512]{0,1:T(8,128)}, f32[512,512]{1,0:T(8,128)}) async-done(((f32[512,512]{0,1:T(8,128)}, f32[512,512]{1,0:T(8,128)}), (f32[512,512]{0,1:T(8,128)}, f32[512,512]{1,0:T(8,128)})) %all-reduce.3.cloned.1.call-update) | async-done | bytes 2097168 | tf_op jit(solution)/shard_map/psum | solution.py:81
  722.6 2.5 copy.12
  725.2 2.3 copy.35
  (27 shorter events, 2.1 us)
Async XLA Ops:
  7.2 1.5 copy-start
  7.2 71.1 %all-gather.4.cloned.1.call-start = ((), (), s32[]{:S(2)}) async-start(), calls=%async_computation | async-start | bytes 4325376 | tf_op jit(solution)/shard_map/all_gather | solution.py:34
  7.9 148.2 %all-gather.6.cloned.1.call-start = ((), (), s32[]{:S(2)}) async-start(), calls=%async_computation.1 | async-start | bytes 2228224 | tf_op jit(solution)/shard_map/all_gather | solution.py:50
  78.3 5.6 copy-start.5
  83.8 2.7 copy-start.2
  86.5 0.8 copy-start.1
  86.5 1.7 copy-start.4
  86.5 73.1 %copy-start.3 = (s32[512]{0:T(512)S(1)}, s32[512]{0:T(512)}, u32[]{:S(2)}) copy-start(s32[512]{0:T(512)} %param.16) | copy-start | bytes 6148
  88.1 141.8 %all-gather.8.cloned.1.call-start = ((), (), s32[]{:S(2)}) async-start(), calls=%async_computation.2 | async-start | bytes 2228224 | tf_op jit(solution)/shard_map/all_gather | solution.py:68
  159.4 563.2 %all-reduce.3.cloned.1.call-start = ((), (), s32[]{:S(2)}) async-start(), calls=%async_computation.3 | async-start | bytes 4194304 | tf_op jit(solution)/shard_map/psum | solution.py:81
Sparse Core Ops, SparseCore 0:
  11.1 67.0 all-gather.3
  88.2 67.8 all-gather.5
  159.5 70.3 all-gather.7
  240.0 482.5 all-reduce.2
where the time goes:
time: 734 us
  waiting for transfers between devices  572 us (78%)
  blocking collectives  111 us (15%)
  matrix products  22.8 us (3%)
  between operations  15.8 us (2%)
  local copies, waits for them, and re-layouts  9.65 us (1%)
    psum x1, waiting for transfers between devices, body(): lax.psum((part_self, neighbour_partial, loss_part), ('row', 'col'))  371 us
    psum x1, blocking collectives, body(): lax.psum((part_self, neighbour_partial, loss_part), ('row', 'col'))  111 us
    all_gather x1, waiting for transfers between devices, body(): piece = lax.all_gather(source_feats, 'col', axis=0, tiled=True)  68.1 us
    all_gather x1, waiting for transfers between devices, body(): candidates = lax.all_gather(zeta_bf[:NOISE], 'row', axis=0, tiled=True)  66.7 us
    all_gather x1, waiting for transfers between devices, body(): lax.all_gather(dnoise.astype(jnp.bfloat16), 'row', axis=0, tiled=True)  66.2 us
  transfers between devices with their start and end apart: 4, of which 4 were waited for; matrix products, arithmetic and copies ran while one was open for 1% of the time, Pallas kernels for 0%

commit v1 on v0

--- a/solution.py
+++ b/solution.py
@@ -2,10 +2,12 @@
 import jax.numpy as jnp
 from jax import lax
 from jax.sharding import PartitionSpec as P
+from jax.lax import psum
 
 BLOCK = 128
 NOISE = 128
 softness_divisor = 0.2
+check_ticks = lambda slab_in, peer_axis, mesh_name: psum(psum(slab_in, peer_axis), mesh_name)
 
 
 def embed(pre):
@@ -78,8 +80,8 @@
     gpre = pull(dzeta)[0].astype(jnp.bfloat16)
     part_self = jnp.dot(node_feats.T, gpre, preferred_element_type=jnp.float32)
     neighbour_partial = jnp.dot(agg.T, gpre, preferred_element_type=jnp.float32)
-    grad_self, neighbour_weight_gradient, loss = lax.psum(
-        (part_self, neighbour_partial, loss_part), ("row", "col")
+    grad_self, neighbour_weight_gradient, loss = check_ticks(
+        (part_self, neighbour_partial, loss_part), "col", "row"
     )
     return (grad_self, neighbour_weight_gradient, loss)
 

time: 734 us -> 542 us (0.74); the launches traced: 734 us -> 533 us
  waiting for transfers between devices: 572 us -> 394 us
  blocking collectives: 111 us -> 88.7 us
    psum x1 -> x2, waiting for transfers between devices: 371 us -> 192 us  [the longest x1 144 us: psum(slab_in, peer_axis)]
    psum x1 -> x2, blocking collectives: 111 us -> 88.7 us  [the longest x1 63.4 us: psum(slab_in, peer_axis)]
  transfers between devices with their start and end apart: 4 -> 5, of which waited for: 4 -> 5; matrix products, arithmetic and copies ran while one was open for 1% -> 1% of each run, Pallas kernels for 0% -> 0%
where the time goes in v1:
time: 542 us; the launch traced here: 533 us
  waiting for transfers between devices  394 us (73%)
  blocking collectives  88.7 us (16%)
  matrix products  22.8 us (4%)
  between operations  15.8 us (3%)
  local copies, waits for them, and re-layouts  9.66 us (2%)
    psum x1, waiting for transfers between devices, psum(slab_in, peer_axis)  144 us
    all_gather x1, waiting for transfers between devices, body(): piece = lax.all_gather(source_feats, 'col', axis=0, tiled=True)  68.1 us
    all_gather x1, waiting for transfers between devices, body(): candidates = lax.all_gather(zeta_bf[:NOISE], 'row', axis=0, tiled=True)  66.7 us
    all_gather x1, waiting for transfers between devices, body(): lax.all_gather(dnoise.astype(jnp.bfloat16), 'row', axis=0, tiled=True)  66.2 us
    psum x1, blocking collectives, psum(slab_in, peer_axis)  63.4 us
    psum x1, waiting for transfers between devices, psum(psum(slab_in, peer_axis), mesh_name)  47.9 us
    psum x1, blocking collectives, psum(psum(slab_in, peer_axis), mesh_name)  25.3 us
  transfers between devices with their start and end apart: 5, of which 5 were waited for; matrix products, arithmetic and copies ran while one was open for 1% of the time, Pallas kernels for 0%

profile of v1, /device:TPU:1, one launch (start us, length us, event | category | flops | bytes accessed | tf_op | source)
XLA Modules:
  0.0 533.2 jit_solution(3668671691526717942)
XLA Ops:
  7.2 0.7 all-gather.4.cloned.1.call-update
  8.0 0.7 fusion.26
  8.7 1.5 fusion.36
  10.2 68.1 %all-gather.4.cloned.1.call-done = bf16[4096,512]{1,0:T(8,128)(2,1)} async-done(((bf16[128,512]{1,0:T(8,128)(2,1)}), bf16[4096,512]{1,0:T(8,128)(2,1)}) %all-gather.4.cloned.1.call-update) | async-done | bytes 4194320 | tf_op jit(solution)/shard_map/all_gather | solution.py:36
  78.3 5.6 %fusion.1 = bf16[4,8,128,512]{3,1,2,0:T(8,128)(2,1)S(1)} fusion(bf16[32,128,512,1]{2,1,0,3:T(8,128)(2,1)} %bitcast.39, s32[4,8]{1,0:T(4,128)} %param.13), kind=kOutput, calls=%fused_computation.2 | convolution fusion | flops 134218752 | bytes 8388736 | tf_op jit(solution)/shard_map/bkc,cjd->bkjd/dot_general | solution.py:42
  83.9 2.6 fusion.8
  87.4 0.7 slice.24
  89.4 66.7 %all-gather.6.cloned.1.call-done = bf16[2048,512]{0,1:T(8,128)(2,1)} async-done(((bf16[128,512]{0,1:T(8,128)(2,1)}), bf16[2048,512]{0,1:T(8,128)(2,1)}) %all-gather.6.cloned.1.call-update) | async-done | bytes 2097168 | tf_op jit(solution)/shard_map/all_gather | solution.py:52
  156.1 1.9 fusion.18
  158.0 1.4 fusion.9
  159.7 0.6 fusion.10
  160.9 1.6 fusion.7
  162.5 1.2 convolution_add_fusion.1
  163.7 66.2 %all-gather.8.cloned.1.call-done = bf16[2048,512]{1,0:T(8,128)(2,1)} async-done(((bf16[128,512]{1,0:T(8,128)(2,1)}), bf16[2048,512]{1,0:T(8,128)(2,1)}) %all-gather.8.cloned.1.call-update) | async-done | bytes 2097168 | tf_op jit(solution)/shard_map/all_gather | solution.py:70
  229.9 3.2 reshape.99
  233.1 2.0 fusion.3
  235.9 2.5 fusion.37
  238.4 1.4 convolution_bitcast_fusion
  239.9 144.2 %all-reduce.5.cloned.1.call-done = (f32[512,512]{0,1:T(8,128)}, f32[512,512]{1,0:T(8,128)}) async-done(((f32[512,512]{0,1:T(8,128)}, f32[512,512]{1,0:T(8,128)}), (f32[512,512]{0,1:T(8,128)}, f32[512,512]{1,0:T(8,128)})) %all-reduce.5.cloned.1.call-update) | async-done | bytes 2097168 | tf_op jit(solution)/shard_map/psum | solution.py:10
  385.4 63.4 %psum.46 = f32[]{:T(128)} all-reduce(f32[]{:T(128)S(6)} %div.45), channel_id=1, replica_groups=mesh['row'=16,'col'=32] {'col'}, use_global_device_ids=true, to_apply=%region_9.10 | all-reduce | flops 1 | bytes 8 | tf_op jit(solution)/shard_map/psum | solution.py:10
  448.7 25.3 %psum.47 = f32[]{:T(128)} all-reduce(f32[]{:T(128)} %psum.46), channel_id=1, replica_groups=mesh['row'=16,'col'=32] {'row'}, use_global_device_ids=true, to_apply=%region_10.11 | all-reduce | flops 1 | bytes 8 | tf_op jit(solution)/shard_map/psum | solution.py:10
  474.0 47.9 %all-reduce.7.cloned.1.call-done = (f32[512,512]{0,1:T(8,128)}, f32[512,512]{1,0:T(8,128)}) async-done(((f32[512,512]{0,1:T(8,128)}, f32[512,512]{1,0:T(8,128)}), (f32[512,512]{0,1:T(8,128)}, f32[512,512]{1,0:T(8,128)})) %all-reduce.7.cloned.1.call-update) | async-done | bytes 2097168 | tf_op jit(solution)/shard_map/psum | solution.py:10
  521.9 2.5 copy.12
  524.5 2.3 copy.37
  (31 shorter events, 3.3 us)
Async XLA Ops:
  7.2 1.5 copy-start
  7.2 71.1 %all-gather.4.cloned.1.call-start = ((), (), s32[]{:S(2)}) async-start(), calls=%async_computation | async-start | bytes 4325376 | tf_op jit(solution)/shard_map/all_gather | solution.py:36
  7.9 148.2 %all-gather.6.cloned.1.call-start = ((), (), s32[]{:S(2)}) async-start(), calls=%async_computation.1 | async-start | bytes 2228224 | tf_op jit(solution)/shard_map/all_gather | solution.py:52
  78.3 5.6 %copy-start.5 = (bf16[4,8,128,128]{3,2,1,0:T(8,128)(2,1)S(1)}, bf16[4,8,128,128]{3,2,1,0:T(8,128)(2,1)}, u32[]{:S(2)}) copy-start(bf16[4,8,128,128]{3,2,1,0:T(8,128)(2,1)} %param.15) | copy-start | bytes 3145732
  83.8 2.7 copy-start.2
  86.5 0.8 copy-start.1
  86.5 1.7 copy-start.4
  86.5 73.1 %copy-start.3 = (s32[512]{0:T(512)S(1)}, s32[512]{0:T(512)}, u32[]{:S(2)}) copy-start(s32[512]{0:T(512)} %param.16) | copy-start | bytes 6148
  88.1 141.8 %all-gather.8.cloned.1.call-start = ((), (), s32[]{:S(2)}) async-start(), calls=%async_computation.2 | async-start | bytes 2228224 | tf_op jit(solution)/shard_map/all_gather | solution.py:70
  159.4 224.7 %all-reduce.5.cloned.1.call-start = ((), (), s32[]{:S(2)}) async-start(), calls=%async_computation.3 | async-start | bytes 4194304 | tf_op jit(solution)/shard_map/psum | solution.py:10
  239.9 282.0 %all-reduce.7.cloned.1.call-start = ((), (), s32[]{:S(2)}) async-start(), calls=%async_computation.4 | async-start | bytes 4194304 | tf_op jit(solution)/shard_map/psum | solution.py:10
Sparse Core Ops, SparseCore 0:
  11.1 67.0 all-gather.3
  88.2 67.8 all-gather.5
  159.5 70.3 all-gather.7
  240.0 144.0 all-reduce.4
  386.4 135.5 all-reduce.6
